TPU v7x, 512 devices: a whole 4x4x16 slice. The times are simulated.
512 devices in a mesh: row: 64 (over z, x), rep: 8 (over y, core).
Axes of the slice: x: 4, y: 4, z: 16, core: 2. Of those that a mesh axis runs over, the one named last changes fastest.
Arguments:
- features: bfloat16 [16384, 128], P('row', 'rep'), may hold values from -6 to 6
- owner_index: int32 [16384], P('row'), may hold values from 0 to 16383, as said below
- block_cols: int32 [128, 64], P('row', 'rep'), may hold values from 0 to 127, as said below
- block_count: int32 [128], P('row'), may hold values from 1 to 64, as said below
- tiles: bfloat16 [128, 64, 128, 128], P('row', 'rep'), may hold values from -0.109375 to 0.109375
- weight: bfloat16 [128, 256], P(None, 'rep'), may hold values from -0.75 to 0.75
- bias: float32 [256], P('rep'), may hold values from -4 to 4
- grad_out: bfloat16 [16384, 256], P('row', 'rep'), may hold values from -6 to 6
Outputs:
- hidden: bfloat16 [16384, 256], P('row', 'rep')
- weight_grad: float32 [128, 256], P(None, 'rep')
- bias_grad: float32 [256], P('rep')
Inputs may be any that keep to these rules, and one draw needn't show every extreme that they name: `owner_index`: A permutation; the 256 rows of each loader shard hold exactly 4 positions of every partition's 2*128 rows. `block_cols`: the block columns of one block row are distinct. Block column c belongs to partition c // 2. Over all slots of one partition's 2 block rows, exactly 1 distinct block columns of each partition are named. `block_count`: some block row has all 64 slots live.
All inputs are finite; a program needn't handle non-finite values.
Results may differ from a plain program's by a relative error of at most 0.017.
Values may be sent and summed in bfloat16 or wider, within the bound.
No kernel may reach another device: no remote copies, remote signals or barrier semaphores. Data moves between devices by JAX's collectives and lax.ppermute only.
A program may use at most 64 MiB of HBM per device.

v0:
```python
import jax
import jax.numpy as jnp
from jax import lax
from jax.sharding import PartitionSpec as P


def block_product(tile_set, col_set, live, table, rows_part):
    size_blk = tile_set.shape[2]
    width = table.shape[1]
    blocks = table.reshape(table.shape[0] // size_blk, size_blk, width)
    picked = blocks[col_set]
    picked = jnp.where(live[:, :, None, None], picked, jnp.zeros_like(picked))
    summed = jnp.einsum("rkij,rkjc->ric", tile_set, picked, preferred_element_type=jnp.float32)
    return summed.reshape(rows_part, width)


def on_device(features, owner_index, block_cols, block_count, tiles, weight, bias, grad_out):
    rows_part = features.shape[0]
    cols_dev = features.shape[1]
    parts_count = lax.axis_size("row")
    per_pair = rows_part // parts_count
    destination = owner_index // rows_part
    order = jnp.argsort(destination, stable=True)
    send_rows = features[order].reshape(parts_count, per_pair, cols_dev)
    send_pos = (owner_index[order] % rows_part).reshape(parts_count, per_pair)
    got_rows, got_pos = (
        lax.all_to_all(send_rows, "row", split_axis=0, concat_axis=0, tiled=True),
        lax.all_to_all(send_pos, "row", split_axis=0, concat_axis=0, tiled=True),
    )
    owned = (
        jnp.zeros((rows_part, cols_dev), jnp.bfloat16)
        .at[got_pos.reshape(rows_part)]
        .set(got_rows.reshape(rows_part, cols_dev))
    )
    wide_own = lax.all_gather(owned, "rep", axis=1, tiled=True)
    table = lax.all_gather(wide_own, "row", axis=0, tiled=True)
    slots_dev = block_cols.shape[1]
    slot_ids = lax.axis_index("rep") * slots_dev + jnp.arange(slots_dev, dtype=jnp.int32)
    live = slot_ids[None, :] < block_count[:, None]
    partial_agg = block_product(tiles, block_cols, live, table, rows_part)
    agg = lax.psum(partial_agg.astype(jnp.bfloat16), "rep")
    pre = jnp.dot(agg, weight, preferred_element_type=jnp.float32) + bias
    hidden = jax.nn.silu(pre).astype(jnp.bfloat16)
    sig = jax.nn.sigmoid(pre)
    dpre = (grad_out.astype(jnp.float32) * sig * (1.0 + pre * (1.0 - sig))).astype(jnp.bfloat16)
    weight_term = jnp.dot(agg.T, dpre, preferred_element_type=jnp.float32)
    bias_term = jnp.sum(dpre.astype(jnp.float32), axis=0)
    weight_grad, bias_grad = lax.psum((weight_term, bias_term), "row")
    return (hidden, weight_grad, bias_grad)


def solution(mesh):
    placed = (
        P("row", "rep"),
        P("row"),
        P("row", "rep"),
        P("row"),
        P("row", "rep", None, None),
        P(None, "rep"),
        P("rep"),
        P("row", "rep"),
    )
    return jax.shard_map(
        on_device,
        mesh=mesh,
        in_specs=placed,
        out_specs=(P("row", "rep"), P(None, "rep"), P("rep")),
        check_vma=False,
    )
```

profile of v0, /device:TPU:8, one launch (start us, length us, event | category | flops | bytes accessed | tf_op | source)
XLA Modules:
  0.0 583.7 jit_solution(2200357898452502559)
XLA Ops:
  7.2 0.0 copy-start
  7.2 0.7 and_select_fusion
  7.9 3.2 sort.17
  11.1 2.0 gather_fusion
  13.1 0.1 gather.12
  13.2 0.6 add_select_fusion
  13.8 18.6 %all-to-all-start = ((s32[64,1,4]{2,1,0:T(1,128)}), s32[64,1,4]{2,1,0:T(1,128)S(1)}, u32[]{:S(2)}, u32[]{:S(2)}) async-start(s32[64,1,4]{2,1,0:T(1,128)} %bitcast), calls=%async_computation | async-start | bytes 65536 | tf_op jit(solution)/shard_map/all_to_all | solution.py:28
  32.4 0.8 copy.18
  33.2 1.5 gather_fusion.1
  34.7 12.5 %all-to-all-done = s32[64,1,4]{2,1,0:T(1,128)S(1)} async-done(((s32[64,1,4]{2,1,0:T(1,128)}), s32[64,1,4]{2,1,0:T(1,128)S(1)}, u32[]{:S(2)}, u32[]{:S(2)}) %all-to-all-start) | async-done | bytes 1056 | tf_op jit(solution)/shard_map/all_to_all | solution.py:28
  47.2 4.6 all-to-all-start.1
  51.8 0.0 all-gather.2.cloned.1.call-start
  51.8 0.5 broadcast.122
  52.3 0.7 reduce.3
  53.1 0.1 reshape.138
  53.2 13.9 %all-to-all-done.1 = bf16[64,4,16]{2,1,0:T(4,128)(2,1)S(1)} async-done(((bf16[64,4,16]{2,1,0:T(4,128)(2,1)}), bf16[64,4,16]{2,1,0:T(4,128)(2,1)S(1)}, u32[]{:S(2)}, u32[]{:S(2)}) %all-to-all-start.1) | async-done | bytes 8224 | tf_op jit(solution)/shard_map/all_to_all | solution.py:27
  67.1 1.2 scatter_custom_fusion
  68.2 0.1 copy.19
  68.3 14.0 %all_gather.6 = bf16[256,128]{0,1:T(8,128)(2,1)} all-gather(bf16[256,16]{0,1:T(8,128)(2,1)S(1)} %copy.19), channel_id=1, replica_groups=mesh['row'=64,'rep'=8] {'rep'}, dimensions={1}, use_global_device_ids=true | all-gather | bytes 73728 | tf_op jit(solution)/shard_map/all_gather | solution.py:35
  82.3 0.0 all-gather.2.cloned.1.call-update
  82.4 0.0 all-reduce.3.cloned.1.call-start
  82.4 0.7 compare_select_fusion.1
  83.1 0.1 reshape.160
  83.2 0.7 broadcast_compare_fusion
  83.9 0.0 copy-start.1
  83.9 0.0 copy-start.2
  83.9 0.0 copy-start.3
  83.9 133.4 %all-gather.2.cloned.1.call-done = bf16[16384,128]{0,1:T(8,128)(2,1)} async-done(((bf16[256,128]{0,1:T(8,128)(2,1)}), bf16[16384,128]{0,1:T(8,128)(2,1)}) %all-gather.2.cloned.1.call-update) | async-done | bytes 4194320 | tf_op jit(solution)/shard_map/all_gather | solution.py:36
  217.4 6.4 %copy.20 = bf16[16384,128]{1,0:T(8,128)(2,1)} copy(bf16[16384,128]{0,1:T(8,128)(2,1)} %all-gather.2.cloned.1.call-done) | data formatting | bytes 8388608 | tf_op jit(solution)/shard_map/all_gather | solution.py:36
  223.7 2.8 gather_fusion.2
  226.6 0.0 copy-done
  226.6 1.0 fusion
  227.6 0.0 all-reduce.3.cloned.1.call-update
  227.6 66.4 %all-reduce.3.cloned.1.call-done = bf16[256,128]{1,0:T(8,128)(2,1)} async-done(((bf16[256,128]{1,0:T(8,128)(2,1)}), bf16[256,128]{1,0:T(8,128)(2,1)}) %all-reduce.3.cloned.1.call-update) | async-done | bytes 65552 | tf_op jit(solution)/shard_map/psum | solution.py:41
  294.0 0.0 copy-done.1
  294.0 0.0 copy-done.2
  294.0 0.0 copy-done.3
  294.0 1.7 convert_reduce_fusion
  295.8 1.0 fusion.8
  296.7 280.1 %all-reduce = (f32[128,32]{0,1:T(8,128)}, f32[32]{0:T(128)}) all-reduce(f32[128,32]{0,1:T(8,128)S(1)} %fusion.8, f32[32]{0:T(128)S(1)} %get-tuple-element.7), channel_id=1, replica_groups=mesh['row'=64,'rep'=8] {'row'}, use_global_device_ids=true, to_apply=%region_3.4 | all-reduce | flops 4128 | bytes 33024 | tf_op jit(solution)/shard_map/psum | solution.py:48
  (6 shorter events, 0.0 us)
Async XLA Ops:
  7.2 219.4 %copy-start = (bf16[2,8,128,128]{3,2,1,0:T(8,128)(2,1)S(1)}, bf16[2,8,128,128]{3,2,1,0:T(8,128)(2,1)}, u32[]{:S(2)}) copy-start(bf16[2,8,128,128]{3,2,1,0:T(8,128)(2,1)} %param.12) | copy-start | bytes 1572868
  13.8 33.3 %all-to-all-start = ((s32[64,1,4]{2,1,0:T(1,128)}), s32[64,1,4]{2,1,0:T(1,128)S(1)}, u32[]{:S(2)}, u32[]{:S(2)}) async-start(s32[64,1,4]{2,1,0:T(1,128)} %bitcast), calls=%async_computation | async-start | bytes 65536 | tf_op jit(solution)/shard_map/all_to_all | solution.py:28
  47.2 19.9 %all-to-all-start.1 = ((bf16[64,4,16]{2,1,0:T(4,128)(2,1)}), bf16[64,4,16]{2,1,0:T(4,128)(2,1)S(1)}, u32[]{:S(2)}, u32[]{:S(2)}) async-start(bf16[64,4,16]{2,1,0:T(4,128)(2,1)} %bitcast.2), calls=%async_computation.1 | async-start | bytes 131072 | tf_op jit(solution)/shard_map/all_to_all | solution.py:27
  51.8 165.6 %all-gather.2.cloned.1.call-start = ((), (), s32[]{:S(2)}) async-start(), calls=%async_computation.2 | async-start | bytes 4259840 | tf_op jit(solution)/shard_map/all_gather | solution.py:36
  82.4 211.7 %all-reduce.3.cloned.1.call-start = ((), (), s32[]{:S(2)}) async-start(), calls=%async_computation.3 | async-start | bytes 131072 | tf_op jit(solution)/shard_map/psum | solution.py:41
  83.9 210.1 %copy-start.1 = (bf16[256,32]{0,1:T(8,128)(2,1)S(1)}, bf16[256,32]{0,1:T(8,128)(2,1)}, u32[]{:S(2)}) copy-start(bf16[256,32]{0,1:T(8,128)(2,1)} %param.15) | copy-start | bytes 49156
  83.9 210.1 %copy-start.2 = (bf16[128,32]{0,1:T(8,128)(2,1)S(1)}, bf16[128,32]{0,1:T(8,128)(2,1)}, u32[]{:S(2)}) copy-start(bf16[128,32]{0,1:T(8,128)(2,1)} %param.13) | copy-start | bytes 24580
  83.9 210.1 %copy-start.3 = (f32[32]{0:T(128)S(1)}, f32[32]{0:T(128)}, u32[]{:S(2)}) copy-start(f32[32]{0:T(128)} %param.14) | copy-start | bytes 388
Sparse Core Ops, SparseCore 0:
  82.5 134.8 all-gather.1
  227.7 66.2 all-reduce.2
where the time goes:
time: 584 us
  blocking collectives  294 us (50%)
  waiting for transfers between devices  226 us (39%)
  starting transfers between devices  23.3 us (4%)
  local copies, waits for them, and re-layouts  15.5 us (3%)
  between operations  14.1 us (2%)
  other arithmetic  6.69 us (1%)
    psum x1, blocking collectives, on_device(): weight_grad, bias_grad = lax.psum((weight_term, bias_term), 'row')  280 us
    all_gather x1, waiting for transfers between devices, on_device(): table = lax.all_gather(wide_own, 'row', axis=0, tiled=True)  133 us
    psum x1, waiting for transfers between devices, on_device(): agg = lax.psum(partial_agg.astype(jnp.bfloat16), 'rep')  66.4 us
    all_to_all x1, starting transfers between devices, on_device(): lax.all_to_all(send_pos, 'row', split_axis=0, concat_axis=0, tiled=True)  18.6 us
    all_gather x1, blocking collectives, on_device(): wide_own = lax.all_gather(owned, 'rep', axis=1, tiled=True)  14 us
    all_to_all x1, waiting for transfers between devices, on_device(): lax.all_to_all(send_rows, 'row', split_axis=0, concat_axis=0, tiled=True)  13.9 us
    all_to_all x1, waiting for transfers between devices, on_device(): lax.all_to_all(send_pos, 'row', split_axis=0, concat_axis=0, tiled=True)  12.5 us
  transfers between devices with their start and end apart: 4, of which 4 were waited for; matrix products, arithmetic and copies ran while one was open for 1% of the time, Pallas kernels for 0%

commit v1 on v0

--- a/solution.py
+++ b/solution.py
@@ -2,6 +2,12 @@
 import jax.numpy as jnp
 from jax import lax
 from jax.sharding import PartitionSpec as P
+
+
+def gather_and_add(x, axis):
+    parts = lax.all_gather(x, axis, axis=0, tiled=False)
+    total = parts.sum(axis=0)
+    return total
 
 
 def block_product(tile_set, col_set, live, table, rows_part):
@@ -38,7 +44,7 @@
     slot_ids = lax.axis_index("rep") * slots_dev + jnp.arange(slots_dev, dtype=jnp.int32)
     live = slot_ids[None, :] < block_count[:, None]
     partial_agg = block_product(tiles, block_cols, live, table, rows_part)
-    agg = lax.psum(partial_agg.astype(jnp.bfloat16), "rep")
+    agg = gather_and_add(partial_agg.astype(jnp.bfloat16), "rep")
     pre = jnp.dot(agg, weight, preferred_element_type=jnp.float32) + bias
     hidden = jax.nn.silu(pre).astype(jnp.bfloat16)
     sig = jax.nn.sigmoid(pre)

time: 584 us -> 525 us (0.90)
  waiting for transfers between devices: 226 us -> 160 us
  blocking collectives: 294 us -> 303 us
    psum x1 -> x0, waiting for transfers between devices: 66.4 us -> none  [on_device(): agg = lax.psum(partial_agg.astype(jnp.bfloat16), 'rep')]
    all_gather x0 -> x1, blocking collectives: none -> 13.2 us  [gather_and_add(): parts = lax.all_gather(x, axis, axis=0, tiled=False)]
  transfers between devices with their start and end apart: 4 -> 3, of which waited for: 4 -> 3; matrix products, arithmetic and copies ran while one was open for 1% -> 1% of each run, Pallas kernels for 0% -> 0%
where the time goes in v1:
time: 525 us; the launch traced here: 524 us
  blocking collectives  303 us (58%)
  waiting for transfers between devices  160 us (30%)
  starting transfers between devices  23.2 us (4%)
  local copies, waits for them, and re-layouts  15.5 us (3%)
  between operations  14.2 us (3%)
  other arithmetic  6.77 us (1%)
    psum x1, blocking collectives, on_device(): weight_grad, bias_grad = lax.psum((weight_term, bias_term), 'row')  276 us
    all_gather x1, waiting for transfers between devices, on_device(): table = lax.all_gather(wide_own, 'row', axis=0, tiled=True)  133 us
    all_to_all x1, starting transfers between devices, on_device(): lax.all_to_all(send_pos, 'row', split_axis=0, concat_axis=0, tiled=True)  18.6 us
    all_gather x1, blocking collectives, on_device(): wide_own = lax.all_gather(owned, 'rep', axis=1, tiled=True)  14 us
    all_to_all x1, waiting for transfers between devices, on_device(): lax.all_to_all(send_rows, 'row', split_axis=0, concat_axis=0, tiled=True)  13.9 us
    all_gather x1, blocking collectives, gather_and_add(): parts = lax.all_gather(x, axis, axis=0, tiled=False)  13.2 us
    all_to_all x1, waiting for transfers between devices, on_device(): lax.all_to_all(send_pos, 'row', split_axis=0, concat_axis=0, tiled=True)  12.5 us
  transfers between devices with their start and end apart: 3, of which 3 were waited for; matrix products, arithmetic and copies ran while one was open for 1% of the time, Pallas kernels for 0%

profile of v1, /device:TPU:8, one launch (start us, length us, event | category | flops | bytes accessed | tf_op | source)
XLA Modules:
  0.0 524.3 jit_solution(3482279730385450446)
XLA Ops:
  7.2 0.0 copy-start
  7.2 0.7 and_select_fusion
  7.9 3.2 sort.17
  11.1 2.0 gather_fusion
  13.1 0.1 gather.12
  13.2 0.6 add_select_fusion
  13.8 18.6 %all-to-all-start = ((s32[64,1,4]{2,1,0:T(1,128)}), s32[64,1,4]{2,1,0:T(1,128)S(1)}, u32[]{:S(2)}, u32[]{:S(2)}) async-start(s32[64,1,4]{2,1,0:T(1,128)} %bitcast), calls=%async_computation | async-start | bytes 65536 | tf_op jit(solution)/shard_map/all_to_all | solution.py:34
  32.4 0.8 copy.18
  33.2 1.5 gather_fusion.1
  34.7 12.5 %all-to-all-done = s32[64,1,4]{2,1,0:T(1,128)S(1)} async-done(((s32[64,1,4]{2,1,0:T(1,128)}), s32[64,1,4]{2,1,0:T(1,128)S(1)}, u32[]{:S(2)}, u32[]{:S(2)}) %all-to-all-start) | async-done | bytes 1056 | tf_op jit(solution)/shard_map/all_to_all | solution.py:34
  47.2 4.6 all-to-all-start.1
  51.8 0.0 all-gather.2.cloned.1.call-start
  51.8 0.5 broadcast.122
  52.3 0.7 reduce.4
  53.1 0.1 reshape.148
  53.2 13.9 %all-to-all-done.1 = bf16[64,4,16]{2,1,0:T(4,128)(2,1)S(1)} async-done(((bf16[64,4,16]{2,1,0:T(4,128)(2,1)}), bf16[64,4,16]{2,1,0:T(4,128)(2,1)S(1)}, u32[]{:S(2)}, u32[]{:S(2)}) %all-to-all-start.1) | async-done | bytes 8224 | tf_op jit(solution)/shard_map/all_to_all | solution.py:33
  67.1 1.2 scatter_custom_fusion
  68.2 0.1 copy.19
  68.3 14.0 %all_gather.10 = bf16[256,128]{0,1:T(8,128)(2,1)} all-gather(bf16[256,16]{0,1:T(8,128)(2,1)S(1)} %copy.19), channel_id=1, replica_groups=mesh['row'=64,'rep'=8] {'rep'}, dimensions={1}, use_global_device_ids=true | all-gather | bytes 73728 | tf_op jit(solution)/shard_map/all_gather | solution.py:41
  82.3 0.0 all-gather.2.cloned.1.call-update
  82.4 0.7 compare_select_fusion.1
  83.1 0.1 reshape.170
  83.2 0.7 broadcast_compare_fusion
  83.9 0.0 copy-start.1
  83.9 0.0 copy-start.2
  83.9 0.0 copy-start.3
  83.9 133.5 %all-gather.2.cloned.1.call-done = bf16[16384,128]{0,1:T(8,128)(2,1)} async-done(((bf16[256,128]{0,1:T(8,128)(2,1)}), bf16[16384,128]{0,1:T(8,128)(2,1)}) %all-gather.2.cloned.1.call-update) | async-done | bytes 4194320 | tf_op jit(solution)/shard_map/all_gather | solution.py:42
  217.4 6.4 %copy.20 = bf16[16384,128]{1,0:T(8,128)(2,1)} copy(bf16[16384,128]{0,1:T(8,128)(2,1)} %all-gather.2.cloned.1.call-done) | data formatting | bytes 8388608 | tf_op jit(solution)/shard_map/all_gather | solution.py:42
  223.7 2.8 gather_fusion.2
  226.6 0.0 copy-done
  226.6 0.4 fusion
  226.9 13.2 %all_gather.12 = bf16[8,256,128]{2,1,0:T(8,128)(2,1)S(1)} all-gather(bf16[1,256,128]{2,1,0:T(8,128)(2,1)S(1)} %bitcast.21), channel_id=1, replica_groups=mesh['row'=64,'rep'=8] {'rep'}, dimensions={0}, use_global_device_ids=true | all-gather | bytes 589824 | tf_op jit(solution)/shard_map/all_gather | solution.py:8
  240.1 0.1 reduce_sum.21
  240.2 0.0 copy-done.1
  240.2 0.0 copy-done.2
  240.2 0.0 copy-done.3
  240.2 0.9 convert_reduce_fusion
  241.1 0.1 fusion.8
  241.2 276.2 %all-reduce = (f32[128,32]{0,1:T(8,128)}, f32[32]{0:T(128)}) all-reduce(f32[128,32]{0,1:T(8,128)S(1)} %fusion.8, f32[32]{0:T(128)S(1)} %get-tuple-element.7), channel_id=1, replica_groups=mesh['row'=64,'rep'=8] {'row'}, use_global_device_ids=true, to_apply=%region_3.4 | all-reduce | flops 4128 | bytes 33024 | tf_op jit(solution)/shard_map/psum | solution.py:54
  (6 shorter events, 0.0 us)
Async XLA Ops:
  7.2 219.4 %copy-start = (bf16[2,8,128,128]{3,2,1,0:T(8,128)(2,1)S(1)}, bf16[2,8,128,128]{3,2,1,0:T(8,128)(2,1)}, u32[]{:S(2)}) copy-start(bf16[2,8,128,128]{3,2,1,0:T(8,128)(2,1)} %param.12) | copy-start | bytes 1572868
  13.8 33.3 %all-to-all-start = ((s32[64,1,4]{2,1,0:T(1,128)}), s32[64,1,4]{2,1,0:T(1,128)S(1)}, u32[]{:S(2)}, u32[]{:S(2)}) async-start(s32[64,1,4]{2,1,0:T(1,128)} %bitcast), calls=%async_computation | async-start | bytes 65536 | tf_op jit(solution)/shard_map/all_to_all | solution.py:34
  47.2 19.9 %all-to-all-start.1 = ((bf16[64,4,16]{2,1,0:T(4,128)(2,1)}), bf16[64,4,16]{2,1,0:T(4,128)(2,1)S(1)}, u32[]{:S(2)}, u32[]{:S(2)}) async-start(bf16[64,4,16]{2,1,0:T(4,128)(2,1)} %bitcast.2), calls=%async_computation.1 | async-start | bytes 131072 | tf_op jit(solution)/shard_map/all_to_all | solution.py:33
  51.8 165.6 %all-gather.2.cloned.1.call-start = ((), (), s32[]{:S(2)}) async-start(), calls=%async_computation.2 | async-start | bytes 4259840 | tf_op jit(solution)/shard_map/all_gather | solution.py:42
  83.9 156.3 %copy-start.1 = (bf16[256,32]{0,1:T(8,128)(2,1)S(1)}, bf16[256,32]{0,1:T(8,128)(2,1)}, u32[]{:S(2)}) copy-start(bf16[256,32]{0,1:T(8,128)(2,1)} %param.15) | copy-start | bytes 49156
  83.9 156.3 %copy-start.2 = (bf16[128,32]{0,1:T(8,128)(2,1)S(1)}, bf16[128,32]{0,1:T(8,128)(2,1)}, u32[]{:S(2)}) copy-start(bf16[128,32]{0,1:T(8,128)(2,1)} %param.13) | copy-start | bytes 24580
  83.9 156.3 %copy-start.3 = (f32[32]{0:T(128)S(1)}, f32[32]{0:T(128)}, u32[]{:S(2)}) copy-start(f32[32]{0:T(128)} %param.14) | copy-start | bytes 388
Sparse Core Ops, SparseCore 0:
  82.5 134.8 all-gather.1
